TPU v7x, 512 devices: a whole 4x4x16 slice. The times are simulated.
512 devices in a mesh: wide: 128 (over y, z, core), narrow: 4 (over x).
Axes of the slice: x: 4, y: 4, z: 16, core: 2. Of those that a mesh axis runs over, the one named last changes fastest.
Arguments:
- raw_echo: bfloat16 [2, 4, 1024, 16384], P(None, 'narrow', 'wide'), may hold values from -6 to 6
- range_replica: bfloat16 [2, 4096], replicated, may hold values from -0.0625 to 0.0625
- interp_weight: float32 [8, 1024], replicated, may hold values from -2.5 to 2.5
- band_offset: int32 [16384], P('wide'), may hold values from 0 to 24, as said below
- azimuth_rate: float32 [16384], P('wide'), may hold values from 0.01 to 0.1
- tile_owner: int32 [4, 16], replicated, may hold values from 0 to 3, as said below
Outputs:
- tile_mean: float32 [4, 64, 16384], P('narrow', None, 'wide')
Inputs may be any that keep to these rules, and one draw needn't show every extreme that they name: band_offset reaches 24 in every draw. `tile_owner`: every tile owns at least one block of every group. One tile, the same for every group, owns exactly 8 blocks of every group; no tile owns more than 8 blocks of one group.
All inputs are finite; a program needn't handle non-finite values.
Results may differ from a plain program's by a relative error of at most 0.011.
Values may be sent and summed in bfloat16 or wider, within the bound.
No kernel may reach another device: no remote copies, remote signals or barrier semaphores. Data moves between devices by JAX's collectives and lax.ppermute only.
A program may use at most 64 MiB of HBM per device.

v0:
```python
import math
import jax
import jax.numpy as jnp
from jax import lax
from jax.sharding import PartitionSpec as P

RSPLIT = 128
PUL_DEV = 8
CAP = 8
HALO = 31


def passed_along(shard, axis, by):
    devices = lax.axis_size(axis)
    pairs = [(i, i + by) for i in range(devices) if 0 <= i + by < devices]
    return lax.ppermute(shard, axis, pairs)


def make_table(size, sign):
    index = jnp.arange(size, dtype=jnp.int32)
    product = index[:, None] * index[None, :] % size
    angle = sign * 2.0 * math.pi / size * product.astype(jnp.float32)
    norm = 1.0 / math.sqrt(size)
    return (
        (jnp.cos(angle) * norm).astype(jnp.bfloat16),
        (jnp.sin(angle) * norm).astype(jnp.bfloat16),
    )


def make_twiddle(first, second, sign):
    heads = jnp.arange(first, dtype=jnp.int32)
    tails = jnp.arange(second, dtype=jnp.int32)
    product = heads[:, None] * tails[None, :] % (first * second)
    angle = sign * 2.0 * math.pi / (first * second) * product.astype(jnp.float32)
    return (jnp.cos(angle), jnp.sin(angle))


def range_transform(real_part, imag_part, first, sign):
    count = real_part.shape[0]
    length = real_part.shape[1]
    second = length // first
    head_cos, head_sin = make_table(first, sign)
    tail_cos, tail_sin = make_table(second, sign)
    twist_cos, twist_sin = make_twiddle(first, second, sign)
    split_real = real_part.reshape(count, first, second)
    split_imag = imag_part.reshape(count, first, second)

    def section_one(table, values):
        return jnp.einsum("kn,pnm->pkm", table, values, preferred_element_type=jnp.float32)

    mid_real = section_one(head_cos, split_real) - section_one(head_sin, split_imag)
    mid_imag = section_one(head_cos, split_imag) + section_one(head_sin, split_real)
    turn_real = (mid_real * twist_cos - mid_imag * twist_sin).astype(jnp.bfloat16)
    turn_imag = (mid_real * twist_sin + mid_imag * twist_cos).astype(jnp.bfloat16)

    def section_two(table, values):
        return jnp.einsum("pam,km->pka", values, table, preferred_element_type=jnp.float32)

    out_real = section_two(tail_cos, turn_real) - section_two(tail_sin, turn_imag)
    out_imag = section_two(tail_cos, turn_imag) + section_two(tail_sin, turn_real)
    return (out_real.reshape(count, length), out_imag.reshape(count, length))


def pulse_transform(real_part, imag_part, first, sign):
    length = real_part.shape[0]
    width = real_part.shape[1]
    second = length // first
    head_cos, head_sin = make_table(first, sign)
    tail_cos, tail_sin = make_table(second, sign)
    twist_cos, twist_sin = make_twiddle(first, second, sign)
    twist_cos = twist_cos[:, :, None]
    twist_sin = twist_sin[:, :, None]
    split_real = real_part.reshape(first, second, width)
    split_imag = imag_part.reshape(first, second, width)

    def section_one(table, values):
        return jnp.einsum("kn,nmc->kmc", table, values, preferred_element_type=jnp.float32)

    mid_real = section_one(head_cos, split_real) - section_one(head_sin, split_imag)
    mid_imag = section_one(head_cos, split_imag) + section_one(head_sin, split_real)
    turn_real = (mid_real * twist_cos - mid_imag * twist_sin).astype(jnp.bfloat16)
    turn_imag = (mid_real * twist_sin + mid_imag * twist_cos).astype(jnp.bfloat16)

    def section_two(table, values):
        return jnp.einsum("kmc,jm->jkc", values, table, preferred_element_type=jnp.float32)

    out_real = section_two(tail_cos, turn_real) - section_two(tail_sin, turn_imag)
    out_imag = section_two(tail_cos, turn_imag) + section_two(tail_sin, turn_real)
    return (out_real.reshape(length, width), out_imag.reshape(length, width))


def azimuth_spectra(values):
    first_real, first_imag = pulse_transform(values[0, :, 0], values[1, :, 0], PUL_DEV, -1)
    return jnp.stack([first_real.astype(jnp.bfloat16), first_imag.astype(jnp.bfloat16)])[
        :, :, None, :
    ]


def per_device(raw_echo, range_replica, interp_weight, band_offset, azimuth_rate, tile_owner):
    echo = raw_echo[:, 0]
    length = echo.shape[2]
    padded = jnp.pad(range_replica, ((0, 0), (0, length - range_replica.shape[1])))
    replica_real, replica_imag = range_transform(padded[0:1], padded[1:2], RSPLIT, -1)
    scale = math.sqrt(length)
    replica_real = replica_real[0] * scale
    replica_imag = replica_imag[0] * scale
    spec_real, spec_imag = range_transform(echo[0], echo[1], RSPLIT, -1)
    match_real = (spec_real * replica_real + spec_imag * replica_imag).astype(jnp.bfloat16)
    match_imag = (spec_imag * replica_real - spec_real * replica_imag).astype(jnp.bfloat16)
    comp_real, comp_imag = range_transform(match_real, match_imag, RSPLIT, 1)
    compressed = jnp.stack([comp_real.astype(jnp.bfloat16), comp_imag.astype(jnp.bfloat16)])
    devices = lax.axis_size("wide")
    width = length // devices
    local_pulses = compressed.shape[1]
    split_bins = compressed.reshape(2, local_pulses, devices, width)
    doppler = azimuth_spectra(
        lax.all_to_all(split_bins, "wide", split_axis=2, concat_axis=1, tiled=True)
    )[:, :, 0]
    rim = passed_along(doppler[:, :, :HALO], "wide", -1)
    extended = jnp.concatenate([doppler, rim], axis=2)
    pulses = extended.shape[1]
    columns = jnp.arange(width + HALO, dtype=jnp.int32)
    bins = jnp.arange(width, dtype=jnp.int32) + band_offset
    moved_real = jnp.zeros((pulses, width), jnp.float32)
    moved_imag = jnp.zeros((pulses, width), jnp.float32)
    for tap_index in range(interp_weight.shape[0]):
        select = (columns[:, None] == (bins + tap_index)[None, :]).astype(jnp.bfloat16)
        picked = jnp.einsum("xpc,cr->xpr", extended, select, preferred_element_type=jnp.float32)
        weight = interp_weight[tap_index][:, None]
        moved_real = moved_real + weight * picked[0]
        moved_imag = moved_imag + weight * picked[1]
    freq = jnp.arange(pulses, dtype=jnp.int32)
    shifted = ((freq + pulses // 2) % pulses - pulses // 2).astype(jnp.float32) / pulses
    phase = math.pi * (shifted * shifted)[:, None] / azimuth_rate[None, :]
    phase_cos = jnp.cos(phase)
    phase_sin = jnp.sin(phase)
    focus_real = (moved_real * phase_cos - moved_imag * phase_sin).astype(jnp.bfloat16)
    focus_imag = (moved_real * phase_sin + moved_imag * phase_cos).astype(jnp.bfloat16)
    image_real, image_imag = pulse_transform(focus_real, focus_imag, PUL_DEV, 1)
    intensity = (image_real * image_real + image_imag * image_imag).astype(jnp.bfloat16)
    block_count = tile_owner.shape[1]
    block_rows = pulses // block_count
    blocks = intensity.reshape(block_count, block_rows, width)
    tiles = lax.axis_size("narrow")
    group = lax.axis_index("narrow")
    tile_ids = jnp.arange(tiles, dtype=jnp.int32)
    own_row = lax.dynamic_slice_in_dim(tile_owner, group, 1, 0)[0]
    member = (own_row[None, :] == tile_ids[:, None]).astype(jnp.int32)
    counts = jnp.sum(
        (tile_owner[:, :, None] == tile_ids[None, None, :]).astype(jnp.int32), axis=(0, 1)
    )
    own_count = jnp.sum(jnp.where(tile_ids == group, counts, 0)).astype(jnp.float32)
    rank = jnp.cumsum(member, axis=1) - 1
    slots = jnp.arange(CAP, dtype=jnp.int32)
    select_slots = ((member[:, None, :] == 1) & (rank[:, None, :] == slots[None, :, None])).astype(
        jnp.bfloat16
    )
    outgoing = jnp.einsum(
        "tsb,bir->tsir", select_slots, blocks, preferred_element_type=jnp.float32
    ).astype(jnp.bfloat16)
    incoming = lax.all_to_all(outgoing, "narrow", split_axis=0, concat_axis=0, tiled=True)
    summed = jnp.sum(incoming, axis=(0, 1), dtype=jnp.float32)[None]
    return summed / own_count


def solution(mesh):
    return jax.shard_map(
        per_device,
        mesh=mesh,
        in_specs=(P(None, "narrow", "wide", None), P(), P(), P("wide"), P("wide"), P()),
        out_specs=P("narrow", None, "wide"),
        check_vma=False,
    )
```

profile of v0, /device:TPU:9, one launch (start us, length us, event | category | flops | bytes accessed | tf_op | source)
XLA Modules:
  0.0 111.7 jit_solution(6334069500444813462)
XLA Ops:
  0.8 1.1 slice_bitcast_fusion.1
  3.2 0.5 fusion.31
  6.4 0.6 fusion.112
  8.5 0.5 fusion.32
  10.6 0.6 subtract_convert_fusion.3
  13.0 1.1 %copy.222 = bf16[2,8,128,128]{3,1,0,2:T(8,128)(2,1)} copy(bf16[2,8,128,128]{3,2,1,0:T(8,128)(2,1)S(1)} %pad_maximum_fusion.1) | data formatting | bytes 1048576 | tf_op jit(solution)/shard_map/stack | solution.py:111
  14.1 20.1 %all-to-all-start = ((bf16[2,8,128,128]{3,1,0,2:T(8,128)(2,1)}), bf16[2,8,128,128]{3,1,0,2:T(8,128)(2,1)S(1)}, u32[]{:S(2)}, u32[]{:S(2)}) async-start(bf16[2,8,128,128]{3,1,0,2:T(8,128)(2,1)} %copy.222), calls=%async_computation | async-start | bytes 1048576 | tf_op jit(solution)/shard_map/all_to_all | solution.py:117
  36.1 30.7 %all-to-all-done = bf16[2,8,128,128]{3,1,0,2:T(8,128)(2,1)S(1)} async-done(((bf16[2,8,128,128]{3,1,0,2:T(8,128)(2,1)}), bf16[2,8,128,128]{3,1,0,2:T(8,128)(2,1)S(1)}, u32[]{:S(2)}, u32[]{:S(2)}) %all-to-all-start) | async-done | bytes 524320 | tf_op jit(solution)/shard_map/all_to_all | solution.py:117
  70.8 3.3 %collective-permute-start = (bf16[2,1024,31]{1,2,0:T(8,128)(2,1)S(1)}, bf16[2,1024,31]{1,2,0:T(8,128)(2,1)S(1)}, u32[]{:S(2)}, u32[]{:S(2)}) collective-permute-start(bf16[2,1024,31]{1,2,0:T(8,128)(2,1)S(1)} %pad_maximum_fusion.2), channel_id=1, source_target_pairs={{4,0},{8,4},{12,8},{16,12},{20,16},{24,20},{28,24},{32,28},{36,32}... | collective-permute-start | bytes 380936 | tf_op jit(solution)/shard_map/ppermute | solution.py:16
  74.1 3.3 %collective-permute-done = bf16[2,1024,31]{1,2,0:T(8,128)(2,1)S(1)} collective-permute-done((bf16[2,1024,31]{1,2,0:T(8,128)(2,1)S(1)}, bf16[2,1024,31]{1,2,0:T(8,128)(2,1)S(1)}, u32[]{:S(2)}, u32[]{:S(2)}) %collective-permute-start) | collective-permute-done | bytes 127008 | tf_op jit(solution)/shard_map/ppermute | solution.py:16
  77.9 0.5 fusion.68
  78.5 0.5 fusion.71
  79.0 0.5 fusion.74
  80.2 0.5 fusion.80
  80.7 0.5 fusion.83
  81.3 0.5 fusion.86
  81.9 0.6 copy-done.2
  82.5 7.7 %subtract_convert_fusion.1 = (bf16[8,128,128]{2,0,1:T(8,128)(2,1)S(1)}, f32[8,128,128]{2,0,1:T(8,128)S(1)}, f32[8,128,128]{2,0,1:T(8,128)S(1)}) fusion(f32[128]{0:T(128)S(1)} %copy-done.2, f32[8,128]{0,1:T(8,128)S(1)} %copy.253, f32[8,128,128]{2,1,0:T(8,128)S(1)} %bitcast.245, f32[8,128]{0,1:T(8,128)S(1)} %copy.251, f32[8,128,128]{2,1,0:T(8,128)S(1)} %bitcast.243, ...), kind=kLoop, calls=%fused_computation.74 | loop fusion | flops 4587520 | bytes 9736704 | tf_op jit(solution)/shard_map/convert_element_type | solution.py:137
  90.4 2.5 %add_convert_fusion.1 = bf16[8,128,128]{2,0,1:T(8,128)(2,1)S(1)} fusion(f32[8,128,128]{2,0,1:T(8,128)S(1)} %get-tuple-element.9, f32[8,128,128]{2,0,1:T(8,128)S(1)} %get-tuple-element.8, f32[128]{0:T(128)S(1)} %copy-done.2, f32[8,128]{0,1:T(8,128)S(1)} %copy.253), kind=kLoop, calls=%fused_computation.73 | loop fusion | flops 655360 | bytes 1315328 | tf_op jit(solution)/shard_map/convert_element_type | solution.py:138
  95.9 1.1 convolution_convert_fusion
  97.0 4.0 %all-to-all-start.1 = ((bf16[4,8,64,128]{3,1,2,0:T(8,128)(2,1)}), bf16[4,8,64,128]{3,1,2,0:T(8,128)(2,1)S(1)}, u32[]{:S(2)}, u32[]{:S(2)}) async-start(bf16[4,8,64,128]{3,1,2,0:T(8,128)(2,1)} %convolution_convert_fusion), calls=%async_computation.1 | async-start | bytes 1048576 | tf_op jit(solution)/shard_map/all_to_all | solution.py:161
  101.1 0.6 fusion.191
  102.4 8.6 %all-to-all-done.1 = bf16[4,8,64,128]{3,1,2,0:T(8,128)(2,1)S(1)} async-done(((bf16[4,8,64,128]{3,1,2,0:T(8,128)(2,1)}), bf16[4,8,64,128]{3,1,2,0:T(8,128)(2,1)S(1)}, u32[]{:S(2)}, u32[]{:S(2)}) %all-to-all-start.1) | async-done | bytes 524320 | tf_op jit(solution)/shard_map/all_to_all | solution.py:161
  111.1 0.6 divide_bitcast_fusion
  (96 shorter events, 20.2 us)
Async XLA Ops:
  4.2 0.9 copy-start.1
  13.0 21.5 %copy-start = (f32[8,1024]{1,0:T(8,128)S(1)}, f32[8,1024]{1,0:T(8,128)}, u32[]{:S(2)}) copy-start(f32[8,1024]{1,0:T(8,128)} %param.8) | copy-start | bytes 98308
  14.1 21.7 %copy-start.3 = (s32[4,16]{1,0:T(4,128)S(1)}, s32[4,16]{1,0:T(4,128)}, u32[]{:S(2)}) copy-start(s32[4,16]{1,0:T(4,128)} %param.11) | copy-start | bytes 772
  14.1 21.9 %copy-start.4 = (s32[128]{0:T(128)S(1)}, s32[128]{0:T(128)}, u32[]{:S(2)}) copy-start(s32[128]{0:T(128)} %param.9) | copy-start | bytes 1540
  14.1 52.7 %all-to-all-start = ((bf16[2,8,128,128]{3,1,0,2:T(8,128)(2,1)}), bf16[2,8,128,128]{3,1,0,2:T(8,128)(2,1)S(1)}, u32[]{:S(2)}, u32[]{:S(2)}) async-start(bf16[2,8,128,128]{3,1,0,2:T(8,128)(2,1)} %copy.222), calls=%async_computation | async-start | bytes 1048576 | tf_op jit(solution)/shard_map/all_to_all | solution.py:117
  70.8 6.6 %collective-permute-start = (bf16[2,1024,31]{1,2,0:T(8,128)(2,1)S(1)}, bf16[2,1024,31]{1,2,0:T(8,128)(2,1)S(1)}, u32[]{:S(2)}, u32[]{:S(2)}) collective-permute-start(bf16[2,1024,31]{1,2,0:T(8,128)(2,1)S(1)} %pad_maximum_fusion.2), channel_id=1, source_target_pairs={{4,0},{8,4},{12,8},{16,12},{20,16},{24,20},{28,24},{32,28},{36,32}... | collective-permute-start | bytes 380936 | tf_op jit(solution)/shard_map/ppermute | solution.py:16
  81.8 0.7 copy-start.2
  97.0 14.0 %all-to-all-start.1 = ((bf16[4,8,64,128]{3,1,2,0:T(8,128)(2,1)}), bf16[4,8,64,128]{3,1,2,0:T(8,128)(2,1)S(1)}, u32[]{:S(2)}, u32[]{:S(2)}) async-start(bf16[4,8,64,128]{3,1,2,0:T(8,128)(2,1)} %convolution_convert_fusion), calls=%async_computation.1 | async-start | bytes 1048576 | tf_op jit(solution)/shard_map/all_to_all | solution.py:161
where the time goes:
time: 112 us
  waiting for transfers between devices  42.6 us (38%)
  starting transfers between devices  27.4 us (24%)
  matrix products  21.6 us (19%)
  other arithmetic  13 us (12%)
  local copies, waits for them, and re-layouts  5.95 us (5%)
  between operations  1.22 us (1%)
    all_to_all x1, waiting for transfers between devices, per_device(): lax.all_to_all(split_bins, 'wide', split_axis=2, concat_axis=1, tiled=True)  30.7 us
    all_to_all x1, starting transfers between devices, per_device(): lax.all_to_all(split_bins, 'wide', split_axis=2, concat_axis=1, tiled=True)  20.1 us
    all_to_all x1, waiting for transfers between devices, per_device(): lax.all_to_all(outgoing, 'narrow', split_axis=0, concat_axis=0, tiled=True)  8.59 us
    convert_element_type x1, other arithmetic, per_device(): (moved_real * phase_cos - moved_imag * phase_sin).astype(jnp.bfloat16)  7.7 us
    dot_general x12, matrix products, section_one(): jnp.einsum('kn,pnm->pkm', table, values, preferred_element_type=jnp.float32)  5.54 us
    dot_general x12, matrix products, section_two(): jnp.einsum('pam,km->pka', values, table, preferred_element_type=jnp.float32)  5.01 us
    all_to_all x1, starting transfers between devices, per_device(): lax.all_to_all(outgoing, 'narrow', split_axis=0, concat_axis=0, tiled=True)  3.99 us
    dot_general x8, matrix products, per_device(): jnp.einsum('xpc,cr->xpr', extended, select, preferred_element_type=jnp.fl...  3.83 us
  transfers between devices with their start and end apart: 3, of which 3 were waited for; matrix products, arithmetic and copies ran while one was open for 2% of the time, Pallas kernels for 0%

commit v1 on v0

--- a/solution.py
+++ b/solution.py
@@ -114,7 +114,12 @@
     local_pulses = compressed.shape[1]
     split_bins = compressed.reshape(2, local_pulses, devices, width)
     doppler = azimuth_spectra(
-        lax.all_to_all(split_bins, "wide", split_axis=2, concat_axis=1, tiled=True)
+        jnp.concatenate(
+            lax.all_to_all(
+                jnp.stack(jnp.split(split_bins, lax.axis_size("wide"), axis=2)), "wide", 0, 0
+            ),
+            axis=1,
+        )
     )[:, :, 0]
     rim = passed_along(doppler[:, :, :HALO], "wide", -1)
     extended = jnp.concatenate([doppler, rim], axis=2)

time: 112 us -> 183 us (1.63)
  local copies, waits for them, and re-layouts: 5.95 us -> 79.5 us
  other arithmetic: 13 us -> 9.6 us
    unnamed x11 -> x138, local copies, waits for them, and re-layouts: 1.66 us -> 76.7 us
    convert_element_type x1, other arithmetic: 7.7 us -> 3.15 us  [per_device(): (moved_real * phase_cos - moved_imag * phase_sin).astype(jnp.bfloat16)]
  transfers between devices with their start and end apart: 3 -> 3, of which waited for: 3 -> 3; matrix products, arithmetic and copies ran while one was open for 2% -> 1% of each run, Pallas kernels for 0% -> 0%
where the time goes in v1:
time: 183 us
  local copies, waits for them, and re-layouts  79.5 us (43%)
  waiting for transfers between devices  43.5 us (24%)
  starting transfers between devices  27.2 us (15%)
  matrix products  21.8 us (12%)
  other arithmetic  9.6 us (5%)
    unnamed x138, local copies, waits for them, and re-layouts  76.7 us
    all_to_all x1, waiting for transfers between devices, per_device(): lax.all_to_all(jnp.stack(jnp.split(split_bins, lax.axis_size('wide'), axi...  31.9 us
    all_to_all x1, starting transfers between devices, per_device(): lax.all_to_all(jnp.stack(jnp.split(split_bins, lax.axis_size('wide'), axi...  19.9 us
    all_to_all x1, waiting for transfers between devices, per_device(): lax.all_to_all(outgoing, 'narrow', split_axis=0, concat_axis=0, tiled=True)  8.59 us
    dot_general x12, matrix products, section_one(): jnp.einsum('kn,pnm->pkm', table, values, preferred_element_type=jnp.float32)  5.54 us
    dot_general x12, matrix products, section_two(): jnp.einsum('pam,km->pka', values, table, preferred_element_type=jnp.float32)  5.01 us
    all_to_all x1, starting transfers between devices, per_device(): lax.all_to_all(outgoing, 'narrow', split_axis=0, concat_axis=0, tiled=True)  3.99 us
    dot_general x8, matrix products, per_device(): jnp.einsum('xpc,cr->xpr', extended, select, preferred_element_type=jnp.fl...  3.84 us
  transfers between devices with their start and end apart: 3, of which 3 were waited for; matrix products, arithmetic and copies ran while one was open for 1% of the time, Pallas kernels for 0%

profile of v1, /device:TPU:9, one launch (start us, length us, event | category | flops | bytes accessed | tf_op | source)
XLA Modules:
  0.0 183.0 jit_solution(7247206582401609212)
XLA Ops:
  0.8 1.1 slice_bitcast_fusion.1
  23.3 0.6 constant_dynamic-update-slice_fusion.112
  28.1 0.6 constant_dynamic-update-slice_fusion.104
  45.2 0.6 constant_dynamic-update-slice_fusion.75
  45.8 0.6 constant_dynamic-update-slice_fusion.74
  49.9 0.6 constant_dynamic-update-slice_fusion.67
  55.3 0.6 constant_dynamic-update-slice_fusion.58
  58.2 0.6 constant_dynamic-update-slice_fusion.53
  68.2 0.6 constant_dynamic-update-slice_fusion.36
  72.4 0.6 constant_dynamic-update-slice_fusion.29
  80.1 0.6 constant_dynamic-update-slice_fusion.16
  84.2 0.6 constant_dynamic-update-slice_fusion.9
  89.6 0.6 constant_dynamic-update-slice_fusion
  90.2 19.9 %all-to-all-start = ((bf16[128,2,8,1,128]{4,2,1,3,0:T(8,128)(2,1)}), bf16[128,2,8,1,128]{4,2,1,3,0:T(8,128)(2,1)S(1)}, u32[]{:S(2)}, u32[]{:S(2)}) async-start(bf16[128,2,8,1,128]{4,2,1,3,0:T(8,128)(2,1)} %constant_dynamic-update-slice_fusion), calls=%async_computation | async-start | bytes 1048576 | tf_op jit(solution)/shard_map/all_to_all | solution.py:118
  110.8 31.9 %all-to-all-done = bf16[128,2,8,1,128]{4,2,1,3,0:T(8,128)(2,1)S(1)} async-done(((bf16[128,2,8,1,128]{4,2,1,3,0:T(8,128)(2,1)}), bf16[128,2,8,1,128]{4,2,1,3,0:T(8,128)(2,1)S(1)}, u32[]{:S(2)}, u32[]{:S(2)}) %all-to-all-start) | async-done | bytes 524320 | tf_op jit(solution)/shard_map/all_to_all | solution.py:118
  146.6 3.3 %collective-permute-start = (bf16[2,1024,31]{1,2,0:T(8,128)(2,1)S(1)}, bf16[2,1024,31]{1,2,0:T(8,128)(2,1)S(1)}, u32[]{:S(2)}, u32[]{:S(2)}) collective-permute-start(bf16[2,1024,31]{1,2,0:T(8,128)(2,1)S(1)} %pad_maximum_fusion.1), channel_id=1, source_target_pairs={{4,0},{8,4},{12,8},{16,12},{20,16},{24,20},{28,24},{32,28},{36,32}... | collective-permute-start | bytes 380936 | tf_op jit(solution)/shard_map/ppermute | solution.py:16
  150.2 3.0 %collective-permute-done = bf16[2,1024,31]{1,2,0:T(8,128)(2,1)S(1)} collective-permute-done((bf16[2,1024,31]{1,2,0:T(8,128)(2,1)S(1)}, bf16[2,1024,31]{1,2,0:T(8,128)(2,1)S(1)}, u32[]{:S(2)}, u32[]{:S(2)}) %collective-permute-start) | collective-permute-done | bytes 127008 | tf_op jit(solution)/shard_map/ppermute | solution.py:16
  158.3 3.2 %subtract_convert_fusion.1 = (bf16[8,128,128]{2,1,0:T(8,128)(2,1)S(1)}, f32[8,128,128]{2,1,0:T(8,128)S(1)}, f32[8,128,128]{2,1,0:T(8,128)S(1)}) fusion(f32[128]{0:T(128)S(1)} %copy-done.2, f32[8,128]{1,0:T(8,128)S(1)} %fusion.288, f32[8,128,128]{2,1,0:T(8,128)S(1)} %bitcast.494, f32[8,128]{1,0:T(8,128)S(1)} %bitcast.506, f32[8,128,128]{2,1,0:T(8,128)S(1)} %bitcast.492, ...), kind=kLoop, calls=%fused_computation.296 | loop fusion | flops 4587520 | bytes 9736704 | tf_op jit(solution)/shard_map/convert_element_type | solution.py:142
  161.8 2.3 %add_convert_fusion.1 = bf16[8,128,128]{2,1,0:T(8,128)(2,1)S(1)} fusion(f32[8,128,128]{2,1,0:T(8,128)S(1)} %get-tuple-element.9, f32[8,128,128]{2,1,0:T(8,128)S(1)} %get-tuple-element.8, f32[128]{0:T(128)S(1)} %copy-done.2, f32[8,128]{1,0:T(8,128)S(1)} %fusion.288), kind=kLoop, calls=%fused_computation.295 | loop fusion | flops 655360 | bytes 1315328 | tf_op jit(solution)/shard_map/convert_element_type | solution.py:143
  167.1 1.1 convolution_convert_fusion
  168.2 4.0 %all-to-all-start.1 = ((bf16[4,8,64,128]{3,1,2,0:T(8,128)(2,1)}), bf16[4,8,64,128]{3,1,2,0:T(8,128)(2,1)S(1)}, u32[]{:S(2)}, u32[]{:S(2)}) async-start(bf16[4,8,64,128]{3,1,2,0:T(8,128)(2,1)} %convolution_convert_fusion), calls=%async_computation.1 | async-start | bytes 1048576 | tf_op jit(solution)/shard_map/all_to_all | solution.py:166
  172.3 0.6 fusion.308
  173.6 8.6 %all-to-all-done.1 = bf16[4,8,64,128]{3,1,2,0:T(8,128)(2,1)S(1)} async-done(((bf16[4,8,64,128]{3,1,2,0:T(8,128)(2,1)}), bf16[4,8,64,128]{3,1,2,0:T(8,128)(2,1)S(1)}, u32[]{:S(2)}, u32[]{:S(2)}) %all-to-all-start.1) | async-done | bytes 524320 | tf_op jit(solution)/shard_map/all_to_all | solution.py:166
  182.4 0.6 divide_bitcast_fusion
  (227 shorter events, 94.8 us)
Async XLA Ops:
  4.2 0.9 copy-start.1
  52.9 57.5 %copy-start.3 = (s32[4,16]{1,0:T(4,128)S(1)}, s32[4,16]{1,0:T(4,128)}, u32[]{:S(2)}) copy-start(s32[4,16]{1,0:T(4,128)} %param.11) | copy-start | bytes 772
  54.1 56.7 %copy-start.4 = (s32[128]{0:T(128)S(1)}, s32[128]{0:T(128)}, u32[]{:S(2)}) copy-start(s32[128]{0:T(128)} %param.9) | copy-start | bytes 1540
  54.1 56.7 %copy-start = (f32[8,1024]{1,0:T(8,128)S(1)}, f32[8,1024]{1,0:T(8,128)}, u32[]{:S(2)}) copy-start(f32[8,1024]{1,0:T(8,128)} %param.8) | copy-start | bytes 98308
  90.2 52.5 %all-to-all-start = ((bf16[128,2,8,1,128]{4,2,1,3,0:T(8,128)(2,1)}), bf16[128,2,8,1,128]{4,2,1,3,0:T(8,128)(2,1)S(1)}, u32[]{:S(2)}, u32[]{:S(2)}) async-start(bf16[128,2,8,1,128]{4,2,1,3,0:T(8,128)(2,1)} %constant_dynamic-update-slice_fusion), calls=%async_computation | async-start | bytes 1048576 | tf_op jit(solution)/shard_map/all_to_all | solution.py:118
  146.6 6.6 %collective-permute-start = (bf16[2,1024,31]{1,2,0:T(8,128)(2,1)S(1)}, bf16[2,1024,31]{1,2,0:T(8,128)(2,1)S(1)}, u32[]{:S(2)}, u32[]{:S(2)}) collective-permute-start(bf16[2,1024,31]{1,2,0:T(8,128)(2,1)S(1)} %pad_maximum_fusion.1), channel_id=1, source_target_pairs={{4,0},{8,4},{12,8},{16,12},{20,16},{24,20},{28,24},{32,28},{36,32}... | collective-permute-start | bytes 380936 | tf_op jit(solution)/shard_map/ppermute | solution.py:16
  157.7 0.7 copy-start.2
  168.2 14.0 %all-to-all-start.1 = ((bf16[4,8,64,128]{3,1,2,0:T(8,128)(2,1)}), bf16[4,8,64,128]{3,1,2,0:T(8,128)(2,1)S(1)}, u32[]{:S(2)}, u32[]{:S(2)}) async-start(bf16[4,8,64,128]{3,1,2,0:T(8,128)(2,1)} %convolution_convert_fusion), calls=%async_computation.1 | async-start | bytes 1048576 | tf_op jit(solution)/shard_map/all_to_all | solution.py:166
